TPU v7x, 512 devices: a whole 4x8x8 slice. The times are simulated.
512 devices in a mesh: seq: 128 (over z, y_hi, x, core), head: 4 (over y_lo).
Axes of the slice: x: 4, y: 8 (y_hi: 2, y_lo: 4; y = y_hi * 4 + y_lo), z: 8, core: 2. Of those that a mesh axis runs over, the one named last changes fastest.
Arguments:
- query_rows: bfloat16 [32768, 8, 128], P('seq', 'head'), may hold values from -20 to 20
- key_rows: bfloat16 [32768, 8, 128], P('seq', 'head'), may hold values from -20 to 20
- value_rows: bfloat16 [32768, 8, 128], P('seq', 'head'), may hold values from -6 to 6
- cotangent: bfloat16 [32768, 8, 128], P('seq', 'head'), may hold values from -6 to 6
- norm_gain: float32 [8, 128], P('head'), may hold values from 0.5 to 2
- offsets: int32 [8], P('head'), may hold values from 0 to 31, as said below
Outputs:
- query_grad: bfloat16 [32768, 8, 128], P('seq', 'head')
- key_grad: bfloat16 [32768, 8, 128], P('seq', 'head')
- value_grad: bfloat16 [32768, 8, 128], P('seq', 'head')
Inputs may be any that keep to these rules, and one draw needn't show every extreme that they name: The heads' offsets are distinct.
All inputs are finite; a program needn't handle non-finite values.
Results may differ from a plain program's by a relative error of at most 0.018.
Values may be sent and summed in bfloat16 or wider, within the bound.
No kernel may reach another device: no remote copies, remote signals or barrier semaphores. Data moves between devices by JAX's collectives and lax.ppermute only.
A program may use at most 128 MiB of HBM per device.

v0:
```python
import numpy as np
import jax
import jax.numpy as jnp
from jax import lax
from jax.sharding import Mesh
from jax.sharding import PartitionSpec as P

RATE2 = 4
RATE3 = 16
RATE4 = 32
RATES = (1, RATE2, RATE3, RATE4)
neg_fill = -1e30
epsilon = 1e-05


def pick_rows(source, wanted, stride):
    row_count = source.shape[0] // stride
    shaped = source.reshape((row_count, stride) + source.shape[1:])
    trailing = (1,) * (source.ndim - 2)
    target = wanted.reshape((1, 1, -1) + trailing)
    column = jnp.arange(stride, dtype=jnp.int32).reshape((1, stride, 1) + trailing)
    zeroed = jnp.where(column == target, shaped, jnp.zeros((), source.dtype))
    return jnp.sum(zeroed, axis=1, dtype=source.dtype)


def put_rows(compact, wanted, stride, filler):
    trailing = (1,) * (compact.ndim - 2)
    target = wanted.reshape((1, 1, -1) + trailing)
    column = jnp.arange(stride, dtype=jnp.int32).reshape((1, stride, 1) + trailing)
    spread = jnp.where(column == target, compact[:, None], jnp.asarray(filler, compact.dtype))
    return spread.reshape((compact.shape[0] * stride,) + compact.shape[1:])


def level_plan(tok_dev, seq_count):
    group_rows = tok_dev * seq_count // RATE4
    spans = [max(1, stride * group_rows // tok_dev) for stride in RATES]
    factors = []
    covered = 1
    for span in spans:
        factors.append(span // covered)
        covered = span
    names = tuple(("s%d" % (index + 1) for index in range(len(spans))))
    return (spans, factors, names)


def shards(plan, query_rows, key_rows, value_rows, cotangent, norm_gain, offsets):
    spans, factors, names = plan
    tok_dev, heads_dev, head_size = query_rows.shape
    score_scale = head_size ** (-0.5)
    features = heads_dev * head_size * lax.axis_size("head")
    seq_axes = tuple(reversed(names))
    device = lax.axis_index(seq_axes)
    levels = []
    for index, stride in enumerate(RATES):
        axes = tuple(reversed(names[: index + 1]))
        span = spans[index]
        rows = tok_dev // stride
        wanted = offsets % stride
        place = device % span * rows
        key_sel = pick_rows(key_rows, wanted, stride)
        value_sel = pick_rows(value_rows, wanted, stride)
        query_sel = pick_rows(query_rows, wanted, stride)
        packed = jnp.stack([key_sel, value_sel, query_sel], axis=1)
        gathered = lax.all_gather(packed, axes, axis=0, tiled=True)
        levels.append(
            dict(
                stride=stride,
                axes=axes,
                rows=rows,
                wanted=wanted,
                place=place,
                key_sel=key_sel,
                value_sel=value_sel,
                query_sel=query_sel,
                key_all=gathered[:, 0],
                value_all=gathered[:, 1],
                query_all=gathered[:, 2],
            )
        )
    lse_total = jnp.full((tok_dev, heads_dev), neg_fill, jnp.float32)
    for level in levels:
        total_rows = level["key_all"].shape[0]
        raw = (
            jnp.einsum(
                "qhd,khd->hqk",
                level["query_sel"],
                level["key_all"],
                preferred_element_type=jnp.float32,
            )
            * score_scale
        )
        query_at = level["place"] + jnp.arange(level["rows"], dtype=jnp.int32)
        key_at = jnp.arange(total_rows, dtype=jnp.int32)
        linked = key_at[None, :] <= query_at[:, None]
        scores = jnp.where(linked[None], raw, neg_fill)
        row_peak = jnp.max(scores, axis=2)
        level_lse = row_peak + jnp.log(jnp.sum(jnp.exp(scores - row_peak[:, :, None]), axis=2))
        level["scores"] = scores
        lse_total = jnp.logaddexp(
            lse_total, put_rows(level_lse.T, level["wanted"], level["stride"], neg_fill)
        )
    attended = jnp.zeros((tok_dev, heads_dev, head_size), jnp.float32)
    for level in levels:
        lse_sel = pick_rows(lse_total, level["wanted"], level["stride"])
        weights = jnp.exp(level["scores"] - lse_sel.T[:, :, None])
        level["lse_sel"] = lse_sel
        level["weights"] = weights
        out_sel = jnp.einsum(
            "hqk,khd->qhd",
            weights.astype(jnp.bfloat16),
            level["value_all"],
            preferred_element_type=jnp.float32,
        )
        attended = attended + put_rows(out_sel, level["wanted"], level["stride"], 0.0)
    grad_in = cotangent.astype(jnp.float32) * norm_gain[None]
    sums = lax.psum(
        jnp.stack(
            [
                jnp.sum(attended, axis=(1, 2)),
                jnp.sum(attended * attended, axis=(1, 2)),
                jnp.sum(grad_in, axis=(1, 2)),
                jnp.sum(grad_in * attended, axis=(1, 2)),
            ]
        ),
        "head",
    )
    centre = sums[0] / features
    variance = sums[1] / features - centre * centre
    inverse = lax.rsqrt(variance + epsilon)
    first_mean = sums[2] / features
    second_mean = inverse * (sums[3] / features - centre * first_mean)
    normed = (attended - centre[:, None, None]) * inverse[:, None, None]
    d_attended = (
        inverse[:, None, None]
        * (grad_in - first_mean[:, None, None] - normed * second_mean[:, None, None])
    ).astype(jnp.bfloat16)
    row_delta = jnp.sum(d_attended.astype(jnp.float32) * attended, axis=2)
    query_grad = jnp.zeros((tok_dev, heads_dev, head_size), jnp.float32)
    for level in levels:
        dout_sel = pick_rows(d_attended, level["wanted"], level["stride"])
        delta_sel = pick_rows(row_delta, level["wanted"], level["stride"])
        weight_grad = jnp.einsum(
            "qhd,khd->hqk", dout_sel, level["value_all"], preferred_element_type=jnp.float32
        )
        score_grad = (level["weights"] * (weight_grad - delta_sel.T[:, :, None])).astype(
            jnp.bfloat16
        )
        grad_sel = jnp.einsum(
            "hqk,khd->qhd", score_grad, level["key_all"], preferred_element_type=jnp.float32
        )
        query_grad = query_grad + put_rows(
            grad_sel * score_scale, level["wanted"], level["stride"], 0.0
        )
        level["dout_all"] = lax.all_gather(dout_sel, level["axes"], axis=0, tiled=True)
        stats = jnp.stack([level["lse_sel"], delta_sel], axis=1)
        level["stats_all"] = lax.all_gather(stats, level["axes"], axis=0, tiled=True)
    key_grad = jnp.zeros((tok_dev, heads_dev, head_size), jnp.float32)
    value_grad = jnp.zeros((tok_dev, heads_dev, head_size), jnp.float32)
    for level in levels:
        query_all = level["query_all"]
        dout_all = level["dout_all"]
        lse_all = level["stats_all"][:, 0]
        delta_all = level["stats_all"][:, 1]
        total_rows = query_all.shape[0]
        raw = (
            jnp.einsum(
                "qhd,khd->hqk", query_all, level["key_sel"], preferred_element_type=jnp.float32
            )
            * score_scale
        )
        key_at = level["place"] + jnp.arange(level["rows"], dtype=jnp.int32)
        query_at = jnp.arange(total_rows, dtype=jnp.int32)
        linked = key_at[None, :] <= query_at[:, None]
        scores = jnp.where(linked[None], raw, neg_fill)
        weights = jnp.exp(scores - lse_all.T[:, :, None])
        value_grad_sel = jnp.einsum(
            "hqk,qhd->khd",
            weights.astype(jnp.bfloat16),
            dout_all,
            preferred_element_type=jnp.float32,
        )
        weight_grad = jnp.einsum(
            "qhd,khd->hqk", dout_all, level["value_sel"], preferred_element_type=jnp.float32
        )
        score_grad = (weights * (weight_grad - delta_all.T[:, :, None])).astype(jnp.bfloat16)
        key_grad_sel = jnp.einsum(
            "hqk,qhd->khd", score_grad, query_all, preferred_element_type=jnp.float32
        )
        key_grad = key_grad + put_rows(
            key_grad_sel * score_scale, level["wanted"], level["stride"], 0.0
        )
        value_grad = value_grad + put_rows(value_grad_sel, level["wanted"], level["stride"], 0.0)
    return (
        query_grad.astype(jnp.bfloat16),
        key_grad.astype(jnp.bfloat16),
        value_grad.astype(jnp.bfloat16),
    )


def solution(mesh):
    seq_count = mesh.shape["seq"]
    head_count = mesh.shape["head"]

    def run(query_rows, key_rows, value_rows, cotangent, norm_gain, offsets):
        tok_dev = query_rows.shape[0] // seq_count
        plan = level_plan(tok_dev, seq_count)
        spans, factors, names = plan
        grid = np.asarray(mesh.devices).reshape(tuple(reversed(factors)) + (head_count,))
        sub_mesh = Mesh(grid, tuple(reversed(names)) + ("head",))
        seq_spec = tuple(reversed(names))
        rows_spec = P(seq_spec, "head", None)
        placed = (rows_spec, rows_spec, rows_spec, rows_spec, P("head", None), P("head"))

        def body(*args):
            return shards(plan, *args)

        return jax.shard_map(
            body,
            mesh=sub_mesh,
            in_specs=placed,
            out_specs=(rows_spec, rows_spec, rows_spec),
            check_vma=False,
        )(query_rows, key_rows, value_rows, cotangent, norm_gain, offsets)

    return run
```

profile of v0, /device:TPU:9, one launch (start us, length us, event | category | flops | bytes accessed | tf_op | source)
XLA Modules:
  0.0 1188.4 jit_solution(1432584091598694713)
XLA Ops:
  18.5 26.9 %all-gather.5.cloned.1.call-done = bf16[1024,3,2,128]{3,0,2,1:T(8,128)(2,1)} async-done(((bf16[256,3,2,128]{3,0,2,1:T(8,128)(2,1)}), bf16[1024,3,2,128]{3,0,2,1:T(8,128)(2,1)}) %all-gather.5.cloned.1.call-update) | async-done | bytes 1572880 | tf_op jit(solution)/shard_map/all_gather | solution.py:64
  45.5 1.5 fusion.126
  47.3 66.7 %all-gather.7.cloned.1.call-done = bf16[1024,3,2,128]{3,0,2,1:T(8,128)(2,1)} async-done(((bf16[64,3,2,128]{3,0,2,1:T(8,128)(2,1)}), bf16[1024,3,2,128]{3,0,2,1:T(8,128)(2,1)}) %all-gather.7.cloned.1.call-update) | async-done | bytes 1572880 | tf_op jit(solution)/shard_map/all_gather | solution.py:64
  115.8 121.9 %all-gather.9.cloned.1.call-done = bf16[1024,3,2,128]{3,0,2,1:T(8,128)(2,1)} async-done(((bf16[16,3,2,128]{3,0,2,1:T(8,128)(2,1)}), bf16[1024,3,2,128]{3,0,2,1:T(8,128)(2,1)}) %all-gather.9.cloned.1.call-update) | async-done | bytes 1572880 | tf_op jit(solution)/shard_map/all_gather | solution.py:64
  239.6 105.8 %all-gather.11.cloned.1.call-done = bf16[1024,3,2,128]{3,0,2,1:T(8,128)(2,1)} async-done(((bf16[8,3,2,128]{3,0,2,1:T(8,128)(2,1)}), bf16[1024,3,2,128]{3,0,2,1:T(8,128)(2,1)}) %all-gather.11.cloned.1.call-update) | async-done | bytes 1572880 | tf_op jit(solution)/shard_map/all_gather | solution.py:64
  357.1 1.8 fusion.115
  358.9 6.9 psum.7
  370.8 9.5 all_gather.41
  385.0 5.1 all_gather.40
  399.8 34.2 %all_gather.43 = bf16[1024,2,128]{2,0,1:T(8,128)(2,1)} all-gather(bf16[64,2,128]{2,0,1:T(8,128)(2,1)S(1)} %select_reduce_fusion.2), channel_id=1, replica_groups=mesh['s4'=2,'s3'=4,'s2'=4,'s1'=4,'head'=4] {'s2','s1'}, dimensions={0}, use_global_device_ids=true | all-gather | bytes 557056 | tf_op jit(solution)/shard_map/all_gather | solution.py:154
  434.1 2.3 fusion.43
  438.1 115.1 %all_gather.45 = bf16[1024,2,128]{2,0,1:T(8,128)(2,1)S(1)} all-gather(bf16[16,2,128]{2,0,1:T(8,128)(2,1)} %select_reduce_fusion.1), channel_id=1, replica_groups=mesh['s4'=2,'s3'=4,'s2'=4,'s1'=4,'head'=4] {'s3','s2','s1'}, dimensions={0}, use_global_device_ids=true | all-gather | bytes 532480 | tf_op jit(solution)/shard_map/all_gather | solution.py:154
  553.3 2.2 fusion.57
  556.9 1.8 copy.108
  558.7 226.1 %all_gather.47 = bf16[1024,2,128]{2,0,1:T(8,128)(2,1)} all-gather(bf16[8,2,128]{2,0,1:T(8,128)(2,1)} %select_reduce_fusion), channel_id=1, replica_groups=mesh['s4'=2,'s3'=4,'s2'=4,'s1'=4,'head'=4] {'s4','s3','s2','s1'}, dimensions={0}, use_global_device_ids=true | all-gather | bytes 528384 | tf_op jit(solution)/shard_map/all_gather | solution.py:154
  784.8 2.2 fusion.63
  788.4 1.8 copy.110
  790.2 2.9 fusion.31
  793.1 1.7 copy.130
  794.7 30.1 %all_gather.42 = f32[1024,2,2]{2,1,0:T(2,128)S(1)} all-gather(f32[64,2,2]{2,1,0:T(2,128)} %copy.115), channel_id=1, replica_groups=mesh['s4'=2,'s3'=4,'s2'=4,'s1'=4,'head'=4] {'s2','s1'}, dimensions={0}, use_global_device_ids=true | all-gather | bytes 17408 | tf_op jit(solution)/shard_map/all_gather | solution.py:156
  830.9 115.6 %all_gather.44 = f32[1024,2,2]{2,1,0:T(2,128)S(1)} all-gather(f32[16,2,2]{2,1,0:T(2,128)S(1)} %copy-done.19), channel_id=1, replica_groups=mesh['s4'=2,'s3'=4,'s2'=4,'s1'=4,'head'=4] {'s3','s2','s1'}, dimensions={0}, use_global_device_ids=true | all-gather | bytes 16640 | tf_op jit(solution)/shard_map/all_gather | solution.py:156
  952.4 217.6 %all_gather.46 = f32[1024,2,2]{2,1,0:T(2,128)S(1)} all-gather(f32[8,2,2]{2,1,0:T(2,128)S(1)} %copy-done.21), channel_id=1, replica_groups=mesh['s4'=2,'s3'=4,'s2'=4,'s1'=4,'head'=4] {'s4','s3','s2','s1'}, dimensions={0}, use_global_device_ids=true | all-gather | bytes 16512 | tf_op jit(solution)/shard_map/all_gather | solution.py:156
  1176.0 1.8 subtract_exponential_fusion
  1179.0 2.1 fusion.30
  (247 shorter events, 70.2 us)
Async XLA Ops:
  7.2 5.2 copy-start.3
  7.2 5.2 copy-start.2
  7.2 5.2 copy-start.6
  7.2 38.3 %all-gather.5.cloned.1.call-start = ((), (), s32[]{:S(2)}) async-start(), calls=%async_computation | async-start | bytes 1966080 | tf_op jit(solution)/shard_map/all_gather | solution.py:64
  9.3 6.4 copy-start.16
  10.2 103.7 %all-gather.7.cloned.1.call-start = ((), (), s32[]{:S(2)}) async-start(), calls=%async_computation.1 | async-start | bytes 1671168 | tf_op jit(solution)/shard_map/all_gather | solution.py:64
  10.3 338.5 %copy-start.38 = (pred[4,2]{0,1:T(4,128)(4,1)}, pred[4,2]{0,1:T(4,128)(4,1)S(1)}, u32[]{:S(2)}) copy-start(pred[4,2]{0,1:T(4,128)(4,1)S(1)} %iota_compare_fusion.10) | copy-start | bytes 28
  12.2 225.5 %all-gather.9.cloned.1.call-start = ((), (), s32[]{:S(2)}) async-start(), calls=%async_computation.2 | async-start | bytes 1597440 | tf_op jit(solution)/shard_map/all_gather | solution.py:64
  12.4 337.1 %copy-start.39 = (pred[16,2]{0,1:T(4,128)(4,1)}, pred[16,2]{0,1:T(4,128)(4,1)S(1)}, u32[]{:S(2)}) copy-start(pred[16,2]{0,1:T(4,128)(4,1)S(1)} %iota_compare_fusion.9) | copy-start | bytes 100
  13.3 332.1 %all-gather.11.cloned.1.call-start = ((), (), s32[]{:S(2)}) async-start(), calls=%async_computation.3 | async-start | bytes 1585152 | tf_op jit(solution)/shard_map/all_gather | solution.py:64
  13.4 33.5 %copy-start.40 = (pred[32,2]{0,1:T(4,128)(4,1)}, pred[32,2]{0,1:T(4,128)(4,1)S(1)}, u32[]{:S(2)}) copy-start(pred[32,2]{0,1:T(4,128)(4,1)S(1)} %iota_compare_fusion.8) | copy-start | bytes 196
  14.4 332.7 %copy-start.26 = (pred[256,2]{0,1:T(4,128)(4,1)}, pred[256,2]{0,1:T(4,128)(4,1)S(1)}, u32[]{:S(2)}) copy-start(pred[256,2]{0,1:T(4,128)(4,1)S(1)} %broadcast_in_dim.619) | copy-start | bytes 1540
  15.3 331.7 %copy-start.29 = (pred[256,2]{0,1:T(4,128)(4,1)}, pred[256,2]{0,1:T(4,128)(4,1)S(1)}, u32[]{:S(2)}) copy-start(pred[256,2]{0,1:T(4,128)(4,1)S(1)} %broadcast_in_dim.611) | copy-start | bytes 1540
  15.8 331.4 %copy-start.31 = (pred[256,2]{0,1:T(4,128)(4,1)}, pred[256,2]{0,1:T(4,128)(4,1)S(1)}, u32[]{:S(2)}) copy-start(pred[256,2]{0,1:T(4,128)(4,1)S(1)} %broadcast_in_dim.602) | copy-start | bytes 1540
  239.1 113.5 %copy-start.7 = (f32[2,16,1024]{2,1,0:T(8,128)}, f32[2,16,1024]{2,1,0:T(8,128)S(1)}, u32[]{:S(2)}) copy-start(f32[2,16,1024]{2,1,0:T(8,128)S(1)} %get-tuple-element.59) | copy-start | bytes 393220
  346.7 8.1 copy-start.14
  350.3 4.4 copy-start.23
  350.3 4.4 copy-start.41
  352.5 4.5 copy-start.27
  357.0 8.8 copy-start.46
  366.0 3.6 copy-start.4
  399.8 34.3 %copy-start.15 = (bf16[64,2,128]{2,0,1:T(8,128)(2,1)}, bf16[64,2,128]{2,0,1:T(8,128)(2,1)S(1)}, u32[]{:S(2)}) copy-start(bf16[64,2,128]{2,0,1:T(8,128)(2,1)S(1)} %select_reduce_fusion.2) | copy-start | bytes 98308
  434.0 119.2 %copy-start.8 = (f32[2,16,1024]{2,1,0:T(8,128)S(1)}, f32[2,16,1024]{2,1,0:T(8,128)}, u32[]{:S(2)}) copy-start(f32[2,16,1024]{2,1,0:T(8,128)} %copy-done.7) | copy-start | bytes 393220
  556.9 233.3 %copy-start.5 = (bf16[256,2,128]{0,2,1:T(8,128)(2,1)S(1)}, bf16[256,2,128]{0,2,1:T(8,128)(2,1)}, u32[]{:S(2)}) copy-start(bf16[256,2,128]{0,2,1:T(8,128)(2,1)} %copy-done.4) | copy-start | bytes 393220
  (32 other events, 60.4 us)
Sparse Core Ops, SparseCore 0:
  10.3 35.1 all-gather.4
  49.4 64.4 all-gather.6
  116.6 121.0 all-gather.8
  242.8 102.5 all-gather.10
where the time goes:
time: 1190 us
  blocking collectives  760 us (64%)
  waiting for transfers between devices  321 us (27%)
  local copies, waits for them, and re-layouts  37.1 us (3%)
  matrix products  34.1 us (3%)
  other arithmetic  20.9 us (2%)
  between operations  14.5 us (1%)
    all_gather x4, blocking collectives, shards(): lax.all_gather(dout_sel, level['axes'], axis=0, tiled=True)  385 us
    all_gather x4, blocking collectives, shards(): lax.all_gather(stats, level['axes'], axis=0, tiled=True)  368 us
    all_gather x4, waiting for transfers between devices, shards(): gathered = lax.all_gather(packed, axes, axis=0, tiled=True)  321 us
  transfers between devices with their start and end apart: 4, of which 4 were waited for; matrix products, arithmetic and copies ran while one was open for 1% of the time, Pallas kernels for 0%

commit v1 on v0

--- a/solution.py
+++ b/solution.py
@@ -151,7 +151,12 @@
         query_grad = query_grad + put_rows(
             grad_sel * score_scale, level["wanted"], level["stride"], 0.0
         )
-        level["dout_all"] = lax.all_gather(dout_sel, level["axes"], axis=0, tiled=True)
+        level["dout_all"] = jnp.concatenate(
+            lax.all_to_all(
+                jnp.stack([dout_sel] * lax.axis_size(level["axes"])), level["axes"], 0, 0
+            ),
+            axis=0,
+        )
         stats = jnp.stack([level["lse_sel"], delta_sel], axis=1)
         level["stats_all"] = lax.all_gather(stats, level["axes"], axis=0, tiled=True)
     key_grad = jnp.zeros((tok_dev, heads_dev, head_size), jnp.float32)

time: 1190 us -> 884 us (0.74)
  blocking collectives: 760 us -> 391 us
  starting transfers between devices: 0.16 us -> 22.1 us
  waiting for transfers between devices: 321 us -> 342 us
  local copies, waits for them, and re-layouts: 37.1 us -> 52.5 us
    all_gather x4 -> x0, blocking collectives: 385 us -> none  [shards(): lax.all_gather(dout_sel, level['axes'], axis=0, tiled=True)]
    all_to_all x0 -> x4, waiting for transfers between devices: none -> 24.7 us  [shards(): lax.all_to_all(jnp.stack([dout_sel] * lax.axis_size(level['axes'])), leve...]
    all_to_all x0 -> x4, starting transfers between devices: none -> 22 us  [shards(): lax.all_to_all(jnp.stack([dout_sel] * lax.axis_size(level['axes'])), leve...]
    all_gather x4, blocking collectives: 368 us -> 384 us  [shards(): lax.all_gather(stats, level['axes'], axis=0, tiled=True)]
  transfers between devices with their start and end apart: 4 -> 8, of which waited for: 4 -> 6; matrix products, arithmetic and copies ran while one was open for 1% -> 8% of each run, Pallas kernels for 0% -> 0%
where the time goes in v1:
time: 884 us; the launch traced here: 882 us
  blocking collectives  391 us (44%)
  waiting for transfers between devices  342 us (39%)
  local copies, waits for them, and re-layouts  52.5 us (6%)
  matrix products  39 us (4%)
  starting transfers between devices  22.1 us (2%)
  other arithmetic  20.2 us (2%)
  between operations  14.6 us (2%)
    all_gather x4, blocking collectives, shards(): lax.all_gather(stats, level['axes'], axis=0, tiled=True)  384 us
    all_gather x4, waiting for transfers between devices, shards(): gathered = lax.all_gather(packed, axes, axis=0, tiled=True)  317 us
    all_to_all x4, waiting for transfers between devices, shards(): lax.all_to_all(jnp.stack([dout_sel] * lax.axis_size(level['axes'])), leve...  24.7 us
    broadcast_in_dim x45, local copies, waits for them, and re-layouts, put_rows(): jnp.where(column == target, compact[:, None], jnp.asarray(filler, compact...  24.6 us
    all_to_all x4, starting transfers between devices, shards(): lax.all_to_all(jnp.stack([dout_sel] * lax.axis_size(level['axes'])), leve...  22 us
  transfers between devices with their start and end apart: 8, of which 6 were waited for; matrix products, arithmetic and copies ran while one was open for 8% of the time, Pallas kernels for 0%

profile of v1, /device:TPU:9, one launch (start us, length us, event | category | flops | bytes accessed | tf_op | source)
XLA Modules:
  0.0 881.9 jit_solution(7838742846553844626)
XLA Ops:
  21.4 24.0 %all-gather.5.cloned.1.call-done = bf16[1024,3,2,128]{3,0,2,1:T(8,128)(2,1)} async-done(((bf16[256,3,2,128]{3,0,2,1:T(8,128)(2,1)}), bf16[1024,3,2,128]{3,0,2,1:T(8,128)(2,1)}) %all-gather.5.cloned.1.call-update) | async-done | bytes 1572880 | tf_op jit(solution)/shard_map/all_gather | solution.py:64
  47.9 66.0 %all-gather.7.cloned.1.call-done = bf16[1024,3,2,128]{3,0,2,1:T(8,128)(2,1)} async-done(((bf16[64,3,2,128]{3,0,2,1:T(8,128)(2,1)}), bf16[1024,3,2,128]{3,0,2,1:T(8,128)(2,1)}) %all-gather.7.cloned.1.call-update) | async-done | bytes 1572880 | tf_op jit(solution)/shard_map/all_gather | solution.py:64
  115.8 121.9 %all-gather.9.cloned.1.call-done = bf16[1024,3,2,128]{3,0,2,1:T(8,128)(2,1)} async-done(((bf16[16,3,2,128]{3,0,2,1:T(8,128)(2,1)}), bf16[1024,3,2,128]{3,0,2,1:T(8,128)(2,1)}) %all-gather.9.cloned.1.call-update) | async-done | bytes 1572880 | tf_op jit(solution)/shard_map/all_gather | solution.py:64
  239.6 105.2 %all-gather.11.cloned.1.call-done = bf16[1024,3,2,128]{3,0,2,1:T(8,128)(2,1)} async-done(((bf16[8,3,2,128]{3,0,2,1:T(8,128)(2,1)}), bf16[1024,3,2,128]{3,0,2,1:T(8,128)(2,1)}) %all-gather.11.cloned.1.call-update) | async-done | bytes 1572880 | tf_op jit(solution)/shard_map/all_gather | solution.py:64
  357.7 6.9 psum.7
  374.3 5.7 all-to-all-start
  380.0 2.2 fusion.63
  382.2 2.2 fusion.57
  384.5 2.3 fusion.43
  386.8 37.1 %all_gather.29 = f32[1024,2,2]{2,1,0:T(2,128)S(1)} all-gather(f32[64,2,2]{2,1,0:T(2,128)} %copy.115), channel_id=1, replica_groups=mesh['s4'=2,'s3'=4,'s2'=4,'s1'=4,'head'=4] {'s2','s1'}, dimensions={0}, use_global_device_ids=true | all-gather | bytes 17408 | tf_op jit(solution)/shard_map/all_gather | solution.py:161
  427.9 3.5 all-to-all-start.1
  446.9 125.7 %all_gather.30 = f32[1024,2,2]{2,1,0:T(2,128)S(1)} all-gather(f32[16,2,2]{2,1,0:T(2,128)} %copy.120), channel_id=1, replica_groups=mesh['s4'=2,'s3'=4,'s2'=4,'s1'=4,'head'=4] {'s3','s2','s1'}, dimensions={0}, use_global_device_ids=true | all-gather | bytes 16640 | tf_op jit(solution)/shard_map/all_gather | solution.py:161
  574.9 216.6 %all_gather.31 = f32[1024,2,2]{2,1,0:T(2,128)S(1)} all-gather(f32[8,2,2]{2,1,0:T(2,128)} %copy.125), channel_id=1, replica_groups=mesh['s4'=2,'s3'=4,'s2'=4,'s1'=4,'head'=4] {'s4','s3','s2','s1'}, dimensions={0}, use_global_device_ids=true | all-gather | bytes 16512 | tf_op jit(solution)/shard_map/all_gather | solution.py:161
  794.0 5.1 all_gather.28
  799.1 2.0 fusion.35
  802.6 5.1 all-to-all-start.2
  809.7 3.1 subtract_exponential_fusion
  812.8 2.2 fusion.31
  815.0 13.9 %all-to-all-done.2 = bf16[64,16,2,128]{3,1,2,0:T(8,128)(2,1)} async-done(((bf16[64,16,2,128]{3,1,2,0:T(8,128)(2,1)}), bf16[64,16,2,128]{3,1,2,0:T(8,128)(2,1)}, u32[]{:S(2)}, u32[]{:S(2)}) %all-to-all-start.2) | async-done | bytes 524320 | tf_op jit(solution)/shard_map/all_to_all | solution.py:155
  830.5 7.7 all-to-all-start.3
  838.2 1.9 fusion.50
  849.9 10.8 %all-to-all-done.3 = bf16[128,8,2,128]{3,1,2,0:T(8,128)(2,1)} async-done(((bf16[128,8,2,128]{3,1,2,0:T(8,128)(2,1)}), bf16[128,8,2,128]{3,1,2,0:T(8,128)(2,1)}, u32[]{:S(2)}, u32[]{:S(2)}) %all-to-all-start.3) | async-done | bytes 524320 | tf_op jit(solution)/shard_map/all_to_all | solution.py:155
  863.8 2.2 fusion.61
  872.6 2.0 fusion.30
  (280 shorter events, 91.9 us)
Async XLA Ops:
  7.2 38.2 %all-gather.5.cloned.1.call-start = ((), (), s32[]{:S(2)}) async-start(), calls=%async_computation.4 | async-start | bytes 1966080 | tf_op jit(solution)/shard_map/all_gather | solution.py:64
  10.2 103.7 %all-gather.7.cloned.1.call-start = ((), (), s32[]{:S(2)}) async-start(), calls=%async_computation.5 | async-start | bytes 1671168 | tf_op jit(solution)/shard_map/all_gather | solution.py:64
  11.6 226.1 %all-gather.9.cloned.1.call-start = ((), (), s32[]{:S(2)}) async-start(), calls=%async_computation.6 | async-start | bytes 1597440 | tf_op jit(solution)/shard_map/all_gather | solution.py:64
  12.7 332.1 %all-gather.11.cloned.1.call-start = ((), (), s32[]{:S(2)}) async-start(), calls=%async_computation.7 | async-start | bytes 1585152 | tf_op jit(solution)/shard_map/all_gather | solution.py:64
  47.8 298.7 %copy-start.24 = (pred[256,2]{0,1:T(4,128)(4,1)S(1)}, pred[256,2]{0,1:T(4,128)(4,1)}, u32[]{:S(2)}) copy-start(pred[256,2]{0,1:T(4,128)(4,1)} %broadcast_in_dim.619) | copy-start | bytes 1540
  47.8 298.7 %copy-start.28 = (pred[256,2]{0,1:T(4,128)(4,1)S(1)}, pred[256,2]{0,1:T(4,128)(4,1)}, u32[]{:S(2)}) copy-start(pred[256,2]{0,1:T(4,128)(4,1)} %broadcast_in_dim.611) | copy-start | bytes 1540
  47.8 298.7 %copy-start.31 = (pred[256,2]{0,1:T(4,128)(4,1)S(1)}, pred[256,2]{0,1:T(4,128)(4,1)}, u32[]{:S(2)}) copy-start(pred[256,2]{0,1:T(4,128)(4,1)} %broadcast_in_dim.602) | copy-start | bytes 1540
  47.8 298.7 %copy-start.55 = (f32[2,256]{1,0:T(2,128)S(1)}, f32[2,256]{1,0:T(2,128)}, u32[]{:S(2)}) copy-start(f32[2,256]{1,0:T(2,128)} %copy-done.54) | copy-start | bytes 6148
  47.9 299.8 %copy-start.19 = (pred[64,4,2]{1,0,2:T(8,128)(4,1)S(1)}, pred[64,4,2]{1,0,2:T(8,128)(4,1)}, u32[]{:S(2)}) copy-start(pred[64,4,2]{1,0,2:T(8,128)(4,1)} %broadcast_in_dim.628) | copy-start | bytes 1540
  47.9 299.8 %copy-start.20 = (pred[64,4,2]{1,0,2:T(8,128)(4,1)S(1)}, pred[64,4,2]{1,0,2:T(8,128)(4,1)}, u32[]{:S(2)}) copy-start(pred[64,4,2]{1,0,2:T(8,128)(4,1)} %broadcast_in_dim.632) | copy-start | bytes 1540
  47.9 299.8 %copy-start.44 = (pred[4,2]{0,1:T(4,128)(4,1)S(1)}, pred[4,2]{0,1:T(4,128)(4,1)}, u32[]{:S(2)}) copy-start(pred[4,2]{0,1:T(4,128)(4,1)} %copy-done.43) | copy-start | bytes 28
  115.3 232.9 %copy-start.42 = (pred[16,16,2]{1,0,2:T(8,128)(4,1)S(1)}, pred[16,16,2]{1,0,2:T(8,128)(4,1)}, u32[]{:S(2)}) copy-start(pred[16,16,2]{1,0,2:T(8,128)(4,1)} %broadcast_in_dim.642) | copy-start | bytes 1540
  115.3 232.9 %copy-start.46 = (pred[16,2]{0,1:T(4,128)(4,1)S(1)}, pred[16,2]{0,1:T(4,128)(4,1)}, u32[]{:S(2)}) copy-start(pred[16,2]{0,1:T(4,128)(4,1)} %copy-done.45) | copy-start | bytes 100
  239.1 118.6 %copy-start.11 = (f32[2,16,1024]{2,1,0:T(8,128)}, f32[2,16,1024]{2,1,0:T(8,128)S(1)}, u32[]{:S(2)}) copy-start(f32[2,16,1024]{2,1,0:T(8,128)S(1)} %get-tuple-element.59) | copy-start | bytes 393220
  374.3 52.5 %all-to-all-start = ((bf16[4,256,2,128]{1,3,2,0:T(8,128)(2,1)}), bf16[4,256,2,128]{1,3,2,0:T(8,128)(2,1)S(1)}, u32[]{:S(2)}, u32[]{:S(2)}) async-start(bf16[4,256,2,128]{1,3,2,0:T(8,128)(2,1)} %stack.83), calls=%async_computation | async-start | bytes 1048576 | tf_op jit(solution)/shard_map/all_to_all | solution.py:155
  384.5 39.4 %copy-start.59 = (f32[8,2]{0,1:T(2,128)S(1)}, f32[8,2]{0,1:T(2,128)}, u32[]{:S(2)}) copy-start(f32[8,2]{0,1:T(2,128)} %select_reduce_fusion.14) | copy-start | bytes 196
  386.8 40.1 %copy-start.16 = (bf16[64,2,128]{2,0,1:T(8,128)(2,1)S(1)}, bf16[64,2,128]{2,0,1:T(8,128)(2,1)}, u32[]{:S(2)}) copy-start(bf16[64,2,128]{2,0,1:T(8,128)(2,1)} %select_reduce_fusion.2) | copy-start | bytes 98308
  427.9 373.2 %all-to-all-start.1 = ((bf16[16,64,2,128]{3,1,2,0:T(8,128)(2,1)}), bf16[16,64,2,128]{3,1,2,0:T(8,128)(2,1)S(1)}, u32[]{:S(2)}, u32[]{:S(2)}) async-start(bf16[16,64,2,128]{3,1,2,0:T(8,128)(2,1)} %stack.87), calls=%async_computation.1 | async-start | bytes 1048576 | tf_op jit(solution)/shard_map/all_to_all | solution.py:155
  802.6 26.3 %all-to-all-start.2 = ((bf16[64,16,2,128]{3,1,2,0:T(8,128)(2,1)}), bf16[64,16,2,128]{3,1,2,0:T(8,128)(2,1)}, u32[]{:S(2)}, u32[]{:S(2)}) async-start(bf16[64,16,2,128]{3,1,2,0:T(8,128)(2,1)} %stack.91), calls=%async_computation.2 | async-start | bytes 1048576 | tf_op jit(solution)/shard_map/all_to_all | solution.py:155
  815.0 23.2 %copy-start.41 = (bf16[8,2,128]{2,0,1:T(8,128)(2,1)S(1)}, bf16[8,2,128]{2,0,1:T(8,128)(2,1)}, u32[]{:S(2)}) copy-start(bf16[8,2,128]{2,0,1:T(8,128)(2,1)} %copy-done.40) | copy-start | bytes 12292
  815.0 23.2 %copy-start.52 = (f32[2,1024]{1,0:T(2,128)S(1)}, f32[2,1024]{1,0:T(2,128)}, u32[]{:S(2)}) copy-start(f32[2,1024]{1,0:T(2,128)} %copy.126) | copy-start | bytes 24580
  815.0 25.9 %copy-start.6 = (f32[1024,1,2]{2,1,0:T(1,128)S(1)}, f32[1024,1,2]{2,1,0:T(1,128)}, u32[]{:S(2)}) copy-start(f32[1024,1,2]{2,1,0:T(1,128)} %get-tuple-element.29) | copy-start | bytes 24580
  815.0 26.7 %copy-start.7 = (f32[1024,1,2]{2,1,0:T(1,128)S(1)}, f32[1024,1,2]{2,1,0:T(1,128)}, u32[]{:S(2)}) copy-start(f32[1024,1,2]{2,1,0:T(1,128)} %get-tuple-element.31) | copy-start | bytes 24580
  830.5 30.3 %all-to-all-start.3 = ((bf16[128,8,2,128]{3,1,2,0:T(8,128)(2,1)}), bf16[128,8,2,128]{3,1,2,0:T(8,128)(2,1)}, u32[]{:S(2)}, u32[]{:S(2)}) async-start(bf16[128,8,2,128]{3,1,2,0:T(8,128)(2,1)} %stack.95), calls=%async_computation.3 | async-start | bytes 1048576 | tf_op jit(solution)/shard_map/all_to_all | solution.py:155
  (47 other events, 300.3 us)
Sparse Core Ops, SparseCore 0:
  10.3 35.1 all-gather.4
  49.4 64.4 all-gather.6
  116.5 121.0 all-gather.8
  242.2 102.5 all-gather.10
